TPU v7x, 32 devices: a whole 2x2x4 slice. The times are simulated.
32 devices in a mesh: row: 16 (over z, y, x), col: 2 (over core).
Axes of the slice: x: 2, y: 2, z: 4, core: 2. Of those that a mesh axis runs over, the one named last changes fastest.
Arguments:
- matrix: bfloat16 [16384, 2048], P('row', 'col'), may hold values from -6 to 6
- fill_mask: int32 [64, 16], P('row', 'col'), may hold values from 0 to 1, as said below
- col_rows: int32 [16], replicated, may hold values from 0 to 127, as said below
- inverses: bfloat16 [2, 128, 128], replicated, may hold values from -0.05 to 0.15625
Outputs:
- factor: bfloat16 [16384, 2048], P('row', 'col')
Inputs may be any that keep to these rules, and one draw needn't show every extreme that they name: `fill_mask`: each column panel's density of filled blocks is drawn for that column from 1/8 to 8/8. `col_rows`: exactly 1 entries lie in each aligned run of 8 slabs.
All inputs are finite; a program needn't handle non-finite values.
Results may differ from a plain program's by a relative error of at most 0.0035.
Values may be sent and summed in bfloat16 or wider, within the bound.
No kernel may reach another device: no remote copies, remote signals or barrier semaphores. Data moves between devices by JAX's collectives and lax.ppermute only.
A program may use at most 64 MiB of HBM per device.

v0:
```python
import jax
import jax.numpy as jnp
from jax import lax
from jax.sharding import PartitionSpec as P

RB = 256
PW = 128


def from_root(shard, axis, root):
    mine = lax.axis_index(axis) == root
    return lax.psum(jnp.where(mine, shard, jnp.zeros_like(shard)), axis)


def contract(left, right):
    return lax.dot_general(
        left, right, (((1,), (1,)), ((), ())), preferred_element_type=jnp.float32
    )


def fetch_slabs(panel_tiles, col_rows):
    row_count = lax.axis_size("row")
    row_index = lax.axis_index("row")
    col_index = lax.axis_index("col")
    slab_tiles = panel_tiles.reshape(-1, PW, PW)
    per_device = slab_tiles.shape[0]
    all_cols = col_rows.shape[0]
    col_panels = all_cols // lax.axis_size("col")
    owner_row = col_rows // per_device
    slab_place = col_rows % per_device
    per_owner = all_cols // row_count
    position = jnp.arange(all_cols, dtype=jnp.int32)
    earlier = (owner_row[None, :] == owner_row[:, None]) & (position[None, :] < position[:, None])
    slab_rank = jnp.sum(earlier.astype(jnp.int32), axis=1)
    is_owned = (owner_row == row_index).astype(jnp.int32)
    rank_match = (slab_rank[:, None] == jnp.arange(per_owner, dtype=jnp.int32)[None, :]).astype(
        jnp.int32
    ) * is_owned[:, None]
    place_match = (slab_place[:, None] == jnp.arange(per_device, dtype=jnp.int32)[None, :]).astype(
        jnp.int32
    )
    select_table = jnp.dot(rank_match.T, place_match).astype(jnp.bfloat16)
    owned_slabs = jnp.einsum(
        "qs,sij->qij", select_table, slab_tiles, preferred_element_type=jnp.float32
    ).astype(jnp.bfloat16)
    everyone = lax.all_gather(owned_slabs, "row", axis=0, tiled=True)
    wanted_owner = lax.dynamic_slice_in_dim(owner_row, col_index * col_panels, col_panels)
    wanted_rank = lax.dynamic_slice_in_dim(slab_rank, col_index * col_panels, col_panels)
    gather_slot = wanted_owner * per_owner + wanted_rank
    pick_table = (
        gather_slot[:, None] == jnp.arange(row_count * per_owner, dtype=jnp.int32)[None, :]
    ).astype(jnp.bfloat16)
    result = jnp.einsum(
        "tq,qij->tij", pick_table, everyone, preferred_element_type=jnp.float32
    ).astype(jnp.bfloat16)
    return result


def shards(matrix, fill_mask, col_rows, inverses):
    col_index = lax.axis_index("col")
    local_rows = matrix.shape[0]
    width = matrix.shape[1]
    col_panels = fill_mask.shape[1]
    rows_mask = jnp.repeat(fill_mask.astype(jnp.float32), RB, axis=0)
    first_local = (
        jnp.dot(matrix[:, :PW], jnp.triu(inverses[0]), preferred_element_type=jnp.float32)
        * rows_mask[:, 0:1]
    ).astype(jnp.bfloat16)
    first_panel = from_root(first_local, "col", 0)
    diag_first = fetch_slabs(first_panel, col_rows)
    column_sum = matrix[:, :PW].astype(jnp.float32) - contract(first_panel, diag_first[0])
    panel_update = column_sum.astype(jnp.bfloat16)
    second_local = (
        jnp.dot(panel_update, jnp.triu(inverses[1]), preferred_element_type=jnp.float32)
        * rows_mask[:, 0:1]
    ).astype(jnp.bfloat16)
    second_panel = from_root(second_local, "col", 1)
    diag_second = fetch_slabs(second_panel, col_rows)
    both_panels = jnp.concatenate((first_panel, second_panel), axis=1)
    both_diag = jnp.concatenate((diag_first, diag_second), axis=2).reshape(-1, 2 * PW)
    schur_sum = matrix.astype(jnp.float32) - contract(both_panels, both_diag)
    masked = (
        (schur_sum.reshape(local_rows, col_panels, PW) * rows_mask[:, :, None])
        .astype(jnp.bfloat16)
        .reshape(local_rows, width)
    )
    leading = jnp.where(
        col_index == 0, first_panel, jnp.where(col_index == 1, second_panel, masked[:, :PW])
    )
    return jnp.concatenate((leading, masked[:, PW:]), axis=1)


def solution(mesh):
    in_specs = (P("row", "col"), P("row", "col"), P(), P())
    out_specs = P("row", "col")
    return jax.shard_map(shards, mesh=mesh, in_specs=in_specs, out_specs=out_specs, check_vma=False)
```

profile of v0, /device:TPU:0, one launch (start us, length us, event | category | flops | bytes accessed | tf_op | source)
XLA Modules:
  0.0 149.6 jit_solution(10960983689356108654)
XLA Ops:
  6.5 0.0 copy-start.2
  6.5 0.0 all-reduce.3.cloned.1.call-start
  6.5 0.7 convert_element_type.58
  7.3 0.1 broadcast_in_dim.8
  7.3 2.0 %fusion.6 = bf16[1024,128]{0,1:T(8,128)(2,1)} fusion(f32[1024]{0:T(1024)S(1)} %bitcast.68, pred[]{:T(512)S(6)} %eq.32, bf16[1024,1024]{1,0:T(8,128)(2,1)} %param.4, bf16[2,128,128]{2,1,0:T(8,128)(2,1)} %param.7, s32[128]{0:T(128)S(1)} %iota_add_fusion), kind=kOutput, calls=%fused_computation.13 | convolution fusion | flops 33980416 | bytes 561665 | tf_op jit(solution)/shard_map/dot_general | solution.py:66
  9.3 0.0 all-reduce.3.cloned.1.call-update
  9.4 0.0 all-reduce.5.cloned.1.call-start
  9.4 0.7 and_select_fusion.1
  10.1 0.2 convert_reduce_fusion
  10.3 0.1 dynamic-slice_add_fusion
  10.3 0.2 convolution_bitcast_fusion
  10.5 20.1 %all-reduce.3.cloned.1.call-done = bf16[1024,128]{0,1:T(8,128)(2,1)} async-done(((bf16[1024,128]{0,1:T(8,128)(2,1)}), bf16[1024,128]{0,1:T(8,128)(2,1)}) %all-reduce.3.cloned.1.call-update) | async-done | bytes 262160 | tf_op jit(solution)/shard_map/psum | solution.py:12
  30.7 0.0 copy-start
  30.7 1.1 copy.24
  31.8 0.2 fusion.47
  32.0 0.1 copy.20
  32.1 44.0 %all-gather = bf16[2048,128]{1,0:T(8,128)(2,1)S(1)} all-gather(bf16[128,128]{1,0:T(8,128)(2,1)S(1)} %bitcast.66), channel_id=2, replica_groups=mesh['row'=16,'col'=2] {'row'}, dimensions={0}, use_global_device_ids=true | all-gather | bytes 557056 | tf_op jit(solution)/shard_map/all_gather | solution.py:46
  76.1 0.4 convolution_convert_fusion.1
  76.5 0.0 copy-done.2
  76.5 0.0 copy-done
  76.6 2.1 %fusion.4 = bf16[1024,128]{0,1:T(8,128)(2,1)} fusion(bf16[1024,128]{0,1:T(8,128)(2,1)S(1)} %copy-done, f32[1024]{0:T(1024)S(1)} %bitcast.69, pred[]{:T(512)S(6)} %eq.33, bf16[1024,1024]{1,0:T(8,128)(2,1)} %param.4, bf16[1,128,128]{2,0,1:T(2,128)(2,1)S(1)} %slice.31, bf16[2,128,128]{2,1,0:T(8,128)(2,1)S(1)} %copy-done.2, s32[128]{0:T(128)S(1)} %iota_add_fusion), kind=kOutput, calls=%fused_computation.11 | convolution fusion | flops 67928064 | bytes 889345 | tf_op jit(solution)/shard_map/dot_general | solution.py:74
  78.7 0.0 all-reduce.5.cloned.1.call-update
  78.7 2.9 %copy.16 = bf16[1024,1024]{0,1:T(8,128)(2,1)S(1)} copy(bf16[1024,1024]{1,0:T(8,128)(2,1)} %param.4) | data formatting | bytes 4194304 | tf_op args[0]
  81.6 11.4 %all-reduce.5.cloned.1.call-done = bf16[1024,128]{0,1:T(8,128)(2,1)} async-done(((bf16[1024,128]{0,1:T(8,128)(2,1)}), bf16[1024,128]{0,1:T(8,128)(2,1)}) %all-reduce.5.cloned.1.call-update) | async-done | bytes 262160 | tf_op jit(solution)/shard_map/psum | solution.py:12
  93.0 0.0 copy-start.1
  93.0 1.1 copy.25
  94.1 0.2 fusion.48
  94.3 0.1 copy.22
  94.4 44.0 %all-gather.1 = bf16[2048,128]{1,0:T(8,128)(2,1)S(1)} all-gather(bf16[128,128]{1,0:T(8,128)(2,1)S(1)} %bitcast.67), channel_id=3, replica_groups=mesh['row'=16,'col'=2] {'row'}, dimensions={0}, use_global_device_ids=true | all-gather | bytes 557056 | tf_op jit(solution)/shard_map/all_gather | solution.py:46
  138.4 0.4 convolution_convert_fusion
  138.8 0.1 pad_maximum_fusion.1
  138.9 0.1 copy.18
  139.0 0.0 copy-done.1
  139.0 0.7 fusion
  139.8 0.1 slice.33
  139.9 0.1 fusion.13
  140.0 0.2 pad_maximum_fusion
  140.2 2.6 %copy.19 = bf16[1024,1024]{1,0:T(8,128)(2,1)} copy(bf16[1024,1024]{0,1:T(8,128)(2,1)S(1)} %pad_maximum_fusion) | data formatting | bytes 4194304 | tf_op jit(solution)/shard_map/concatenate | solution.py:90
  (3 shorter events, 0.0 us)
Async XLA Ops:
  6.5 70.0 %copy-start.2 = (bf16[2,128,128]{2,1,0:T(8,128)(2,1)S(1)}, bf16[2,128,128]{2,1,0:T(8,128)(2,1)}, u32[]{:S(2)}) copy-start(bf16[2,128,128]{2,1,0:T(8,128)(2,1)} %param.7) | copy-start | bytes 196612
  6.5 24.1 %all-reduce.3.cloned.1.call-start = ((), (), s32[]{:S(2)}) async-start(), calls=%async_computation | async-start | bytes 524288 | tf_op jit(solution)/shard_map/psum | solution.py:12
  9.4 83.7 %all-reduce.5.cloned.1.call-start = ((), (), s32[]{:S(2)}) async-start(), calls=%async_computation.1 | async-start | bytes 524288 | tf_op jit(solution)/shard_map/psum | solution.py:12
  30.7 45.9 %copy-start = (bf16[1024,128]{0,1:T(8,128)(2,1)S(1)}, bf16[1024,128]{0,1:T(8,128)(2,1)}, u32[]{:S(2)}) copy-start(bf16[1024,128]{0,1:T(8,128)(2,1)} %all-reduce.3.cloned.1.call-done) | copy-start | bytes 786436
  93.0 46.0 %copy-start.1 = (bf16[1024,128]{0,1:T(8,128)(2,1)S(1)}, bf16[1024,128]{0,1:T(8,128)(2,1)}, u32[]{:S(2)}) copy-start(bf16[1024,128]{0,1:T(8,128)(2,1)} %all-reduce.5.cloned.1.call-done) | copy-start | bytes 786436
Sparse Core Ops, SparseCore 0:
  9.7 20.9 all-reduce.2
  78.8 14.1 all-reduce.4
where the time goes:
time: 150 us
  blocking collectives  88 us (59%)
  waiting for transfers between devices  31.6 us (21%)
  between operations  13.5 us (9%)
  local copies, waits for them, and re-layouts  8.17 us (5%)
  matrix products  6.28 us (4%)
  other arithmetic  1.96 us (1%)
    all_gather x2, blocking collectives, fetch_slabs(): everyone = lax.all_gather(owned_slabs, 'row', axis=0, tiled=True)  88 us
    psum x2, waiting for transfers between devices, from_root(): return lax.psum(jnp.where(mine, shard, jnp.zeros_like(shard)), axis)  31.6 us
    unnamed x9, local copies, waits for them, and re-layouts  5.01 us
  transfers between devices with their start and end apart: 2, of which 2 were waited for; matrix products, arithmetic and copies ran while one was open for 3% of the time, Pallas kernels for 0%

commit v1 on v0

--- a/solution.py
+++ b/solution.py
@@ -19,6 +19,23 @@
 
 
 def fetch_slabs(panel_tiles, col_rows):
+
+    def _open_squares(frame_in, local_values):
+        net_axis = "row"
+        y, u_next, carry = (lax.psum(1, net_axis), lax.axis_index(net_axis), frame_in.shape[0])
+        kept_rows = list(map(lambda dev_j: (dev_j, (dev_j + 1) % y), range(y)))
+        right_arr = y // 2
+        piece_next = d_next = frame_in
+        log = list(map(lambda dev_j: (dev_j, (dev_j - 1) % y), range(y)))
+        current_arr = local_values(frame_in, u_next * carry)
+        for b in range(1, right_arr + 1):
+            piece_next = lax.ppermute(piece_next, net_axis, kept_rows)
+            if b < y - right_arr:
+                d_next = lax.ppermute(d_next, net_axis, log)
+                current_arr = current_arr + local_values(d_next, (u_next + b) % y * carry)
+            current_arr = current_arr + local_values(piece_next, (u_next - b) % y * carry)
+        return current_arr
+
     row_count = lax.axis_size("row")
     row_index = lax.axis_index("row")
     col_index = lax.axis_index("col")
@@ -43,15 +60,20 @@
     owned_slabs = jnp.einsum(
         "qs,sij->qij", select_table, slab_tiles, preferred_element_type=jnp.float32
     ).astype(jnp.bfloat16)
-    everyone = lax.all_gather(owned_slabs, "row", axis=0, tiled=True)
     wanted_owner = lax.dynamic_slice_in_dim(owner_row, col_index * col_panels, col_panels)
     wanted_rank = lax.dynamic_slice_in_dim(slab_rank, col_index * col_panels, col_panels)
     gather_slot = wanted_owner * per_owner + wanted_rank
     pick_table = (
         gather_slot[:, None] == jnp.arange(row_count * per_owner, dtype=jnp.int32)[None, :]
     ).astype(jnp.bfloat16)
-    result = jnp.einsum(
-        "tq,qij->tij", pick_table, everyone, preferred_element_type=jnp.float32
+    result = _open_squares(
+        owned_slabs,
+        local_values=lambda shard_2, at: jnp.einsum(
+            "tq,qij->tij",
+            lax.dynamic_slice_in_dim(pick_table, at, shard_2.shape[0], axis=1),
+            shard_2,
+            preferred_element_type=jnp.float32,
+        ),
     ).astype(jnp.bfloat16)
     return result
 

time: 150 us -> 197 us (1.31)
  blocking collectives: 88 us -> 0 us
  starting transfers between devices: 0.04 us -> 80.9 us
  waiting for transfers between devices: 31.6 us -> 84.5 us
    all_gather x2 -> x0, blocking collectives: 88 us -> none  [fetch_slabs(): everyone = lax.all_gather(owned_slabs, 'row', axis=0, tiled=True)]
    ppermute x0 -> x30, starting transfers between devices: none -> 80.8 us  [the longest x14 80.6 us: _open_squares(): d_next = lax.ppermute(d_next, net_axis, log)]
    ppermute x0 -> x30, waiting for transfers between devices: none -> 50.3 us  [the longest x16 41.1 us: _open_squares(): piece_next = lax.ppermute(piece_next, net_axis, kept_rows)]
    psum x2, waiting for transfers between devices: 31.6 us -> 34.2 us  [from_root(): return lax.psum(jnp.where(mine, shard, jnp.zeros_like(shard)), axis)]
  transfers between devices with their start and end apart: 2 -> 32, of which waited for: 2 -> 23; matrix products, arithmetic and copies ran while one was open for 3% -> 2% of each run, Pallas kernels for 0% -> 0%
where the time goes in v1:
time: 197 us; the launch traced here: 196 us
  waiting for transfers between devices  84.5 us (43%)
  starting transfers between devices  80.9 us (41%)
  between operations  14 us (7%)
  local copies, waits for them, and re-layouts  7.94 us (4%)
  matrix products  5.49 us (3%)
  other arithmetic  3.53 us (2%)
    ppermute x14, starting transfers between devices, _open_squares(): d_next = lax.ppermute(d_next, net_axis, log)  80.6 us
    ppermute x16, waiting for transfers between devices, _open_squares(): piece_next = lax.ppermute(piece_next, net_axis, kept_rows)  41.1 us
    psum x2, waiting for transfers between devices, from_root(): return lax.psum(jnp.where(mine, shard, jnp.zeros_like(shard)), axis)  34.2 us
    ppermute x14, waiting for transfers between devices, _open_squares(): d_next = lax.ppermute(d_next, net_axis, log)  9.13 us
    unnamed x9, local copies, waits for them, and re-layouts  4.92 us
  transfers between devices with their start and end apart: 32, of which 23 were waited for; matrix products, arithmetic and copies ran while one was open for 2% of the time, Pallas kernels for 0%

profile of v1, /device:TPU:0, one launch (start us, length us, event | category | flops | bytes accessed | tf_op | source)
XLA Modules:
  0.0 196.3 jit_solution(10537926311260747002)
XLA Ops:
  6.5 0.7 convert_element_type.58
  7.3 2.0 %fusion.6 = bf16[1024,128]{0,1:T(8,128)(2,1)} fusion(f32[1024]{0:T(1024)S(1)} %bitcast.190, pred[]{:T(512)S(6)} %eq.115, bf16[1024,1024]{1,0:T(8,128)(2,1)} %param.4, bf16[2,128,128]{2,1,0:T(8,128)(2,1)} %param.7, s32[128]{0:T(128)S(1)} %iota_add_fusion), kind=kOutput, calls=%fused_computation.11 | convolution fusion | flops 33980416 | bytes 561665 | tf_op jit(solution)/shard_map/dot_general | solution.py:88
  9.4 0.7 and_select_fusion.1
  10.1 0.2 convert_reduce_fusion
  10.2 0.2 convolution_bitcast_fusion
  10.8 19.9 %all-reduce.3.cloned.1.call-done = bf16[1024,128]{0,1:T(8,128)(2,1)} async-done(((bf16[1024,128]{0,1:T(8,128)(2,1)}), bf16[1024,128]{0,1:T(8,128)(2,1)}) %all-reduce.3.cloned.1.call-update) | async-done | bytes 262160 | tf_op jit(solution)/shard_map/psum | solution.py:12
  30.7 1.1 copy.14
  31.8 0.2 fusion.72
  32.1 5.5 %collective-permute-start = (bf16[1,128,128]{2,1,0:T(8,128)(2,1)S(1)}, bf16[1,128,128]{2,1,0:T(8,128)(2,1)S(1)}, u32[]{:S(2)}, u32[]{:S(2)}) collective-permute-start(bf16[1,128,128]{2,1,0:T(8,128)(2,1)S(1)} %get-tuple-element.8), channel_id=1, source_target_pairs={{0,30},{2,0},{4,2},{6,4},{8,6},{10,8},{12,10},{14,12},{16,14},{18,... | collective-permute-start | bytes 98312 | tf_op jit(solution)/shard_map/ppermute | solution.py:34
  37.7 1.5 collective-permute-done
  39.2 5.9 %collective-permute-start.2 = (bf16[1,128,128]{2,1,0:T(8,128)(2,1)S(1)}, bf16[1,128,128]{2,1,0:T(8,128)(2,1)S(1)}, u32[]{:S(2)}, u32[]{:S(2)}) collective-permute-start(bf16[1,128,128]{2,1,0:T(8,128)(2,1)S(1)} %collective-permute-done), channel_id=1, source_target_pairs={{0,30},{2,0},{4,2},{6,4},{8,6},{10,8},{12,10},{14,12},{16,14},{18,... | collective-permute-start | bytes 98312 | tf_op jit(solution)/shard_map/ppermute | solution.py:34
  45.2 1.5 collective-permute-done.2
  46.7 5.9 %collective-permute-start.4 = (bf16[1,128,128]{2,1,0:T(8,128)(2,1)S(1)}, bf16[1,128,128]{2,1,0:T(8,128)(2,1)S(1)}, u32[]{:S(2)}, u32[]{:S(2)}) collective-permute-start(bf16[1,128,128]{2,1,0:T(8,128)(2,1)S(1)} %collective-permute-done.2), channel_id=1, source_target_pairs={{0,30},{2,0},{4,2},{6,4},{8,6},{10,8},{12,10},{14,12},{16,14},{18,... | collective-permute-start | bytes 98312 | tf_op jit(solution)/shard_map/ppermute | solution.py:34
  52.7 1.5 collective-permute-done.4
  54.2 5.9 %collective-permute-start.6 = (bf16[1,128,128]{2,1,0:T(8,128)(2,1)S(1)}, bf16[1,128,128]{2,1,0:T(8,128)(2,1)S(1)}, u32[]{:S(2)}, u32[]{:S(2)}) collective-permute-start(bf16[1,128,128]{2,1,0:T(8,128)(2,1)S(1)} %collective-permute-done.4), channel_id=1, source_target_pairs={{0,30},{2,0},{4,2},{6,4},{8,6},{10,8},{12,10},{14,12},{16,14},{18,... | collective-permute-start | bytes 98312 | tf_op jit(solution)/shard_map/ppermute | solution.py:34
  60.2 1.5 collective-permute-done.6
  61.7 5.9 %collective-permute-start.8 = (bf16[1,128,128]{2,1,0:T(8,128)(2,1)S(1)}, bf16[1,128,128]{2,1,0:T(8,128)(2,1)S(1)}, u32[]{:S(2)}, u32[]{:S(2)}) collective-permute-start(bf16[1,128,128]{2,1,0:T(8,128)(2,1)S(1)} %collective-permute-done.6), channel_id=1, source_target_pairs={{0,30},{2,0},{4,2},{6,4},{8,6},{10,8},{12,10},{14,12},{16,14},{18,... | collective-permute-start | bytes 98312 | tf_op jit(solution)/shard_map/ppermute | solution.py:34
  67.7 1.5 collective-permute-done.8
  69.2 5.9 %collective-permute-start.10 = (bf16[1,128,128]{2,1,0:T(8,128)(2,1)S(1)}, bf16[1,128,128]{2,1,0:T(8,128)(2,1)S(1)}, u32[]{:S(2)}, u32[]{:S(2)}) collective-permute-start(bf16[1,128,128]{2,1,0:T(8,128)(2,1)S(1)} %collective-permute-done.8), channel_id=1, source_target_pairs={{0,30},{2,0},{4,2},{6,4},{8,6},{10,8},{12,10},{14,12},{16,14},{18,... | collective-permute-start | bytes 98312 | tf_op jit(solution)/shard_map/ppermute | solution.py:34
  75.2 1.6 collective-permute-done.10
  76.9 6.1 %collective-permute-start.12 = (bf16[1,128,128]{2,1,0:T(8,128)(2,1)S(1)}, bf16[1,128,128]{2,1,0:T(8,128)(2,1)S(1)}, u32[]{:S(2)}, u32[]{:S(2)}) collective-permute-start(bf16[1,128,128]{2,1,0:T(8,128)(2,1)S(1)} %collective-permute-done.10), channel_id=1, source_target_pairs={{0,30},{2,0},{4,2},{6,4},{8,6},{10,8},{12,10},{14,12},{16,14},{18,... | collective-permute-start | bytes 98312 | tf_op jit(solution)/shard_map/ppermute | solution.py:34
  83.0 7.5 %collective-permute-done.13 = bf16[1,128,128]{2,1,0:T(8,128)(2,1)S(1)} collective-permute-done((bf16[1,128,128]{2,1,0:T(8,128)(2,1)S(1)}, bf16[1,128,128]{2,1,0:T(8,128)(2,1)S(1)}, u32[]{:S(2)}, u32[]{:S(2)}) %collective-permute-start.13) | collective-permute-done | bytes 32800 | tf_op jit(solution)/shard_map/ppermute | solution.py:32
  90.5 7.5 %collective-permute-done.14 = bf16[1,128,128]{2,1,0:T(8,128)(2,1)S(1)} collective-permute-done((bf16[1,128,128]{2,1,0:T(8,128)(2,1)S(1)}, bf16[1,128,128]{2,1,0:T(8,128)(2,1)S(1)}, u32[]{:S(2)}, u32[]{:S(2)}) %collective-permute-start.14) | collective-permute-done | bytes 32800 | tf_op jit(solution)/shard_map/ppermute | solution.py:32
  98.0 0.7 add_convert_fusion.1
  98.7 2.1 %fusion.4 = bf16[1024,128]{0,1:T(8,128)(2,1)} fusion(bf16[1024,128]{0,1:T(8,128)(2,1)S(1)} %copy-done, f32[1024]{0:T(1024)S(1)} %bitcast.191, pred[]{:T(512)S(6)} %eq.116, bf16[1024,1024]{1,0:T(8,128)(2,1)} %param.4, bf16[8,128,128]{2,1,0:T(8,128)(2,1)S(1)} %add_convert_fusion.1, bf16[2,128,128]{2,1,0:T(8,128)(2,1)S(1)} %copy-done.2, s32[128]{0:T(128)S(1)} %iota_add_fusion), kind=kOutput, calls=%fused_computation.9 | convolution fusion | flops 67928064 | bytes 856577 | tf_op jit(solution)/shard_map/dot_general | solution.py:96
  100.9 14.3 %all-reduce.5.cloned.1.call-done = bf16[1024,128]{0,1:T(8,128)(2,1)} async-done(((bf16[1024,128]{0,1:T(8,128)(2,1)}), bf16[1024,128]{0,1:T(8,128)(2,1)}) %all-reduce.5.cloned.1.call-update) | async-done | bytes 262160 | tf_op jit(solution)/shard_map/psum | solution.py:12
  115.2 1.0 copy.15
  116.2 0.2 fusion.73
  116.5 5.5 %collective-permute-start.15 = (bf16[1,128,128]{2,1,0:T(8,128)(2,1)S(1)}, bf16[1,128,128]{2,1,0:T(8,128)(2,1)S(1)}, u32[]{:S(2)}, u32[]{:S(2)}) collective-permute-start(bf16[1,128,128]{2,1,0:T(8,128)(2,1)S(1)} %get-tuple-element.6), channel_id=1, source_target_pairs={{0,30},{2,0},{4,2},{6,4},{8,6},{10,8},{12,10},{14,12},{16,14},{18,... | collective-permute-start | bytes 98312 | tf_op jit(solution)/shard_map/ppermute | solution.py:34
  122.0 2.9 %copy.9 = bf16[1024,1024]{0,1:T(8,128)(2,1)S(1)} copy(bf16[1024,1024]{1,0:T(8,128)(2,1)} %param.4) | data formatting | bytes 4194304 | tf_op args[0]
  124.9 5.6 %collective-permute-start.17 = (bf16[1,128,128]{2,1,0:T(8,128)(2,1)S(1)}, bf16[1,128,128]{2,1,0:T(8,128)(2,1)S(1)}, u32[]{:S(2)}, u32[]{:S(2)}) collective-permute-start(bf16[1,128,128]{2,1,0:T(8,128)(2,1)S(1)} %collective-permute-done.15), channel_id=1, source_target_pairs={{0,30},{2,0},{4,2},{6,4},{8,6},{10,8},{12,10},{14,12},{16,14},{18,... | collective-permute-start | bytes 98312 | tf_op jit(solution)/shard_map/ppermute | solution.py:34
  130.5 1.9 collective-permute-done.16
  132.4 5.7 %collective-permute-start.19 = (bf16[1,128,128]{2,1,0:T(8,128)(2,1)S(1)}, bf16[1,128,128]{2,1,0:T(8,128)(2,1)S(1)}, u32[]{:S(2)}, u32[]{:S(2)}) collective-permute-start(bf16[1,128,128]{2,1,0:T(8,128)(2,1)S(1)} %collective-permute-done.17), channel_id=1, source_target_pairs={{0,30},{2,0},{4,2},{6,4},{8,6},{10,8},{12,10},{14,12},{16,14},{18,... | collective-permute-start | bytes 98312 | tf_op jit(solution)/shard_map/ppermute | solution.py:34
  138.1 1.8 collective-permute-done.18
  139.9 5.7 %collective-permute-start.21 = (bf16[1,128,128]{2,1,0:T(8,128)(2,1)S(1)}, bf16[1,128,128]{2,1,0:T(8,128)(2,1)S(1)}, u32[]{:S(2)}, u32[]{:S(2)}) collective-permute-start(bf16[1,128,128]{2,1,0:T(8,128)(2,1)S(1)} %collective-permute-done.19), channel_id=1, source_target_pairs={{0,30},{2,0},{4,2},{6,4},{8,6},{10,8},{12,10},{14,12},{16,14},{18,... | collective-permute-start | bytes 98312 | tf_op jit(solution)/shard_map/ppermute | solution.py:34
  145.6 1.8 collective-permute-done.20
  147.5 5.7 %collective-permute-start.23 = (bf16[1,128,128]{2,1,0:T(8,128)(2,1)S(1)}, bf16[1,128,128]{2,1,0:T(8,128)(2,1)S(1)}, u32[]{:S(2)}, u32[]{:S(2)}) collective-permute-start(bf16[1,128,128]{2,1,0:T(8,128)(2,1)S(1)} %collective-permute-done.21), channel_id=1, source_target_pairs={{0,30},{2,0},{4,2},{6,4},{8,6},{10,8},{12,10},{14,12},{16,14},{18,... | collective-permute-start | bytes 98312 | tf_op jit(solution)/shard_map/ppermute | solution.py:34
  153.2 1.8 collective-permute-done.22
  155.0 5.7 %collective-permute-start.25 = (bf16[1,128,128]{2,1,0:T(8,128)(2,1)S(1)}, bf16[1,128,128]{2,1,0:T(8,128)(2,1)S(1)}, u32[]{:S(2)}, u32[]{:S(2)}) collective-permute-start(bf16[1,128,128]{2,1,0:T(8,128)(2,1)S(1)} %collective-permute-done.23), channel_id=1, source_target_pairs={{0,30},{2,0},{4,2},{6,4},{8,6},{10,8},{12,10},{14,12},{16,14},{18,... | collective-permute-start | bytes 98312 | tf_op jit(solution)/shard_map/ppermute | solution.py:34
  160.7 1.8 collective-permute-done.24
  162.5 5.7 %collective-permute-start.27 = (bf16[1,128,128]{2,1,0:T(8,128)(2,1)S(1)}, bf16[1,128,128]{2,1,0:T(8,128)(2,1)S(1)}, u32[]{:S(2)}, u32[]{:S(2)}) collective-permute-start(bf16[1,128,128]{2,1,0:T(8,128)(2,1)S(1)} %collective-permute-done.25), channel_id=1, source_target_pairs={{0,30},{2,0},{4,2},{6,4},{8,6},{10,8},{12,10},{14,12},{16,14},{18,... | collective-permute-start | bytes 98312 | tf_op jit(solution)/shard_map/ppermute | solution.py:34
  168.2 1.8 collective-permute-done.26
  170.0 7.5 %collective-permute-done.28 = bf16[1,128,128]{2,1,0:T(8,128)(2,1)S(1)} collective-permute-done((bf16[1,128,128]{2,1,0:T(8,128)(2,1)S(1)}, bf16[1,128,128]{2,1,0:T(8,128)(2,1)S(1)}, u32[]{:S(2)}, u32[]{:S(2)}) %collective-permute-start.28) | collective-permute-done | bytes 32800 | tf_op jit(solution)/shard_map/ppermute | solution.py:32
  177.6 7.5 %collective-permute-done.29 = bf16[1,128,128]{2,1,0:T(8,128)(2,1)S(1)} collective-permute-done((bf16[1,128,128]{2,1,0:T(8,128)(2,1)S(1)}, bf16[1,128,128]{2,1,0:T(8,128)(2,1)S(1)}, u32[]{:S(2)}, u32[]{:S(2)}) %collective-permute-start.29) | collective-permute-done | bytes 32800 | tf_op jit(solution)/shard_map/ppermute | solution.py:32
  185.0 0.7 add_convert_fusion
  185.8 0.7 fusion
  186.8 0.2 pad_maximum_fusion
  186.9 2.6 %copy.10 = bf16[1024,1024]{1,0:T(8,128)(2,1)} copy(bf16[1024,1024]{0,1:T(8,128)(2,1)S(1)} %pad_maximum_fusion) | data formatting | bytes 4194304 | tf_op jit(solution)/shard_map/concatenate | solution.py:112
  (83 shorter events, 1.6 us)
Async XLA Ops:
  6.5 24.1 %all-reduce.3.cloned.1.call-start = ((), (), s32[]{:S(2)}) async-start(), calls=%async_computation | async-start | bytes 524288 | tf_op jit(solution)/shard_map/psum | solution.py:12
  9.3 105.8 %all-reduce.5.cloned.1.call-start = ((), (), s32[]{:S(2)}) async-start(), calls=%async_computation.1 | async-start | bytes 524288 | tf_op jit(solution)/shard_map/psum | solution.py:12
  10.6 88.1 %copy-start.2 = (bf16[2,128,128]{2,1,0:T(8,128)(2,1)S(1)}, bf16[2,128,128]{2,1,0:T(8,128)(2,1)}, u32[]{:S(2)}) copy-start(bf16[2,128,128]{2,1,0:T(8,128)(2,1)} %param.7) | copy-start | bytes 196612
  30.7 68.0 %copy-start = (bf16[1024,128]{0,1:T(8,128)(2,1)S(1)}, bf16[1024,128]{0,1:T(8,128)(2,1)}, u32[]{:S(2)}) copy-start(bf16[1024,128]{0,1:T(8,128)(2,1)} %all-reduce.3.cloned.1.call-done) | copy-start | bytes 786436
  32.1 7.1 %collective-permute-start = (bf16[1,128,128]{2,1,0:T(8,128)(2,1)S(1)}, bf16[1,128,128]{2,1,0:T(8,128)(2,1)S(1)}, u32[]{:S(2)}, u32[]{:S(2)}) collective-permute-start(bf16[1,128,128]{2,1,0:T(8,128)(2,1)S(1)} %get-tuple-element.8), channel_id=1, source_target_pairs={{0,30},{2,0},{4,2},{6,4},{8,6},{10,8},{12,10},{14,12},{16,14},{18,... | collective-permute-start | bytes 98312 | tf_op jit(solution)/shard_map/ppermute | solution.py:34
  37.6 7.6 %collective-permute-start.1 = (bf16[1,128,128]{2,1,0:T(8,128)(2,1)S(1)}, bf16[1,128,128]{2,1,0:T(8,128)(2,1)S(1)}, u32[]{:S(2)}, u32[]{:S(2)}) collective-permute-start(bf16[1,128,128]{2,1,0:T(8,128)(2,1)S(1)} %get-tuple-element.8), channel_id=1, source_target_pairs={{0,2},{2,4},{4,6},{6,8},{8,10},{10,12},{12,14},{14,16},{16,18},{18... | collective-permute-start | bytes 98312 | tf_op jit(solution)/shard_map/ppermute | solution.py:32
  39.2 7.5 %collective-permute-start.2 = (bf16[1,128,128]{2,1,0:T(8,128)(2,1)S(1)}, bf16[1,128,128]{2,1,0:T(8,128)(2,1)S(1)}, u32[]{:S(2)}, u32[]{:S(2)}) collective-permute-start(bf16[1,128,128]{2,1,0:T(8,128)(2,1)S(1)} %collective-permute-done), channel_id=1, source_target_pairs={{0,30},{2,0},{4,2},{6,4},{8,6},{10,8},{12,10},{14,12},{16,14},{18,... | collective-permute-start | bytes 98312 | tf_op jit(solution)/shard_map/ppermute | solution.py:34
  45.2 7.5 %collective-permute-start.3 = (bf16[1,128,128]{2,1,0:T(8,128)(2,1)S(1)}, bf16[1,128,128]{2,1,0:T(8,128)(2,1)S(1)}, u32[]{:S(2)}, u32[]{:S(2)}) collective-permute-start(bf16[1,128,128]{2,1,0:T(8,128)(2,1)S(1)} %collective-permute-done.1), channel_id=1, source_target_pairs={{0,2},{2,4},{4,6},{6,8},{8,10},{10,12},{12,14},{14,16},{16,18},{18... | collective-permute-start | bytes 98312 | tf_op jit(solution)/shard_map/ppermute | solution.py:32
  46.7 7.5 %collective-permute-start.4 = (bf16[1,128,128]{2,1,0:T(8,128)(2,1)S(1)}, bf16[1,128,128]{2,1,0:T(8,128)(2,1)S(1)}, u32[]{:S(2)}, u32[]{:S(2)}) collective-permute-start(bf16[1,128,128]{2,1,0:T(8,128)(2,1)S(1)} %collective-permute-done.2), channel_id=1, source_target_pairs={{0,30},{2,0},{4,2},{6,4},{8,6},{10,8},{12,10},{14,12},{16,14},{18,... | collective-permute-start | bytes 98312 | tf_op jit(solution)/shard_map/ppermute | solution.py:34
  52.7 7.5 %collective-permute-start.5 = (bf16[1,128,128]{2,1,0:T(8,128)(2,1)S(1)}, bf16[1,128,128]{2,1,0:T(8,128)(2,1)S(1)}, u32[]{:S(2)}, u32[]{:S(2)}) collective-permute-start(bf16[1,128,128]{2,1,0:T(8,128)(2,1)S(1)} %collective-permute-done.3), channel_id=1, source_target_pairs={{0,2},{2,4},{4,6},{6,8},{8,10},{10,12},{12,14},{14,16},{16,18},{18... | collective-permute-start | bytes 98312 | tf_op jit(solution)/shard_map/ppermute | solution.py:32
  54.2 7.5 %collective-permute-start.6 = (bf16[1,128,128]{2,1,0:T(8,128)(2,1)S(1)}, bf16[1,128,128]{2,1,0:T(8,128)(2,1)S(1)}, u32[]{:S(2)}, u32[]{:S(2)}) collective-permute-start(bf16[1,128,128]{2,1,0:T(8,128)(2,1)S(1)} %collective-permute-done.4), channel_id=1, source_target_pairs={{0,30},{2,0},{4,2},{6,4},{8,6},{10,8},{12,10},{14,12},{16,14},{18,... | collective-permute-start | bytes 98312 | tf_op jit(solution)/shard_map/ppermute | solution.py:34
  60.2 7.5 %collective-permute-start.7 = (bf16[1,128,128]{2,1,0:T(8,128)(2,1)S(1)}, bf16[1,128,128]{2,1,0:T(8,128)(2,1)S(1)}, u32[]{:S(2)}, u32[]{:S(2)}) collective-permute-start(bf16[1,128,128]{2,1,0:T(8,128)(2,1)S(1)} %collective-permute-done.5), channel_id=1, source_target_pairs={{0,2},{2,4},{4,6},{6,8},{8,10},{10,12},{12,14},{14,16},{16,18},{18... | collective-permute-start | bytes 98312 | tf_op jit(solution)/shard_map/ppermute | solution.py:32
  61.7 7.5 %collective-permute-start.8 = (bf16[1,128,128]{2,1,0:T(8,128)(2,1)S(1)}, bf16[1,128,128]{2,1,0:T(8,128)(2,1)S(1)}, u32[]{:S(2)}, u32[]{:S(2)}) collective-permute-start(bf16[1,128,128]{2,1,0:T(8,128)(2,1)S(1)} %collective-permute-done.6), channel_id=1, source_target_pairs={{0,30},{2,0},{4,2},{6,4},{8,6},{10,8},{12,10},{14,12},{16,14},{18,... | collective-permute-start | bytes 98312 | tf_op jit(solution)/shard_map/ppermute | solution.py:34
  67.7 7.5 %collective-permute-start.9 = (bf16[1,128,128]{2,1,0:T(8,128)(2,1)S(1)}, bf16[1,128,128]{2,1,0:T(8,128)(2,1)S(1)}, u32[]{:S(2)}, u32[]{:S(2)}) collective-permute-start(bf16[1,128,128]{2,1,0:T(8,128)(2,1)S(1)} %collective-permute-done.7), channel_id=1, source_target_pairs={{0,2},{2,4},{4,6},{6,8},{8,10},{10,12},{12,14},{14,16},{16,18},{18... | collective-permute-start | bytes 98312 | tf_op jit(solution)/shard_map/ppermute | solution.py:32
  69.2 7.6 %collective-permute-start.10 = (bf16[1,128,128]{2,1,0:T(8,128)(2,1)S(1)}, bf16[1,128,128]{2,1,0:T(8,128)(2,1)S(1)}, u32[]{:S(2)}, u32[]{:S(2)}) collective-permute-start(bf16[1,128,128]{2,1,0:T(8,128)(2,1)S(1)} %collective-permute-done.8), channel_id=1, source_target_pairs={{0,30},{2,0},{4,2},{6,4},{8,6},{10,8},{12,10},{14,12},{16,14},{18,... | collective-permute-start | bytes 98312 | tf_op jit(solution)/shard_map/ppermute | solution.py:34
  75.2 7.7 %collective-permute-start.11 = (bf16[1,128,128]{2,1,0:T(8,128)(2,1)S(1)}, bf16[1,128,128]{2,1,0:T(8,128)(2,1)S(1)}, u32[]{:S(2)}, u32[]{:S(2)}) collective-permute-start(bf16[1,128,128]{2,1,0:T(8,128)(2,1)S(1)} %collective-permute-done.9), channel_id=1, source_target_pairs={{0,2},{2,4},{4,6},{6,8},{8,10},{10,12},{12,14},{14,16},{16,18},{18... | collective-permute-start | bytes 98312 | tf_op jit(solution)/shard_map/ppermute | solution.py:32
  76.9 13.7 %collective-permute-start.12 = (bf16[1,128,128]{2,1,0:T(8,128)(2,1)S(1)}, bf16[1,128,128]{2,1,0:T(8,128)(2,1)S(1)}, u32[]{:S(2)}, u32[]{:S(2)}) collective-permute-start(bf16[1,128,128]{2,1,0:T(8,128)(2,1)S(1)} %collective-permute-done.10), channel_id=1, source_target_pairs={{0,30},{2,0},{4,2},{6,4},{8,6},{10,8},{12,10},{14,12},{16,14},{18,... | collective-permute-start | bytes 98312 | tf_op jit(solution)/shard_map/ppermute | solution.py:34
  82.9 7.6 %collective-permute-start.13 = (bf16[1,128,128]{2,1,0:T(8,128)(2,1)S(1)}, bf16[1,128,128]{2,1,0:T(8,128)(2,1)S(1)}, u32[]{:S(2)}, u32[]{:S(2)}) collective-permute-start(bf16[1,128,128]{2,1,0:T(8,128)(2,1)S(1)} %collective-permute-done.11), channel_id=1, source_target_pairs={{0,2},{2,4},{4,6},{6,8},{8,10},{10,12},{12,14},{14,16},{16,18},{18... | collective-permute-start | bytes 98312 | tf_op jit(solution)/shard_map/ppermute | solution.py:32
  90.5 7.5 %collective-permute-start.14 = (bf16[1,128,128]{2,1,0:T(8,128)(2,1)S(1)}, bf16[1,128,128]{2,1,0:T(8,128)(2,1)S(1)}, u32[]{:S(2)}, u32[]{:S(2)}) collective-permute-start(bf16[1,128,128]{2,1,0:T(8,128)(2,1)S(1)} %collective-permute-done.13), channel_id=1, source_target_pairs={{0,2},{2,4},{4,6},{6,8},{8,10},{10,12},{12,14},{14,16},{16,18},{18... | collective-permute-start | bytes 98312 | tf_op jit(solution)/shard_map/ppermute | solution.py:32
  116.5 8.4 %collective-permute-start.15 = (bf16[1,128,128]{2,1,0:T(8,128)(2,1)S(1)}, bf16[1,128,128]{2,1,0:T(8,128)(2,1)S(1)}, u32[]{:S(2)}, u32[]{:S(2)}) collective-permute-start(bf16[1,128,128]{2,1,0:T(8,128)(2,1)S(1)} %get-tuple-element.6), channel_id=1, source_target_pairs={{0,30},{2,0},{4,2},{6,4},{8,6},{10,8},{12,10},{14,12},{16,14},{18,... | collective-permute-start | bytes 98312 | tf_op jit(solution)/shard_map/ppermute | solution.py:34
  124.8 61.0 %copy-start.1 = (bf16[1024,128]{0,1:T(8,128)(2,1)S(1)}, bf16[1024,128]{0,1:T(8,128)(2,1)}, u32[]{:S(2)}) copy-start(bf16[1024,128]{0,1:T(8,128)(2,1)} %all-reduce.5.cloned.1.call-done) | copy-start | bytes 786436
  124.8 7.6 %collective-permute-start.16 = (bf16[1,128,128]{2,1,0:T(8,128)(2,1)S(1)}, bf16[1,128,128]{2,1,0:T(8,128)(2,1)S(1)}, u32[]{:S(2)}, u32[]{:S(2)}) collective-permute-start(bf16[1,128,128]{2,1,0:T(8,128)(2,1)S(1)} %get-tuple-element.6), channel_id=1, source_target_pairs={{0,2},{2,4},{4,6},{6,8},{8,10},{10,12},{12,14},{14,16},{16,18},{18... | collective-permute-start | bytes 98312 | tf_op jit(solution)/shard_map/ppermute | solution.py:32
  124.9 7.5 %collective-permute-start.17 = (bf16[1,128,128]{2,1,0:T(8,128)(2,1)S(1)}, bf16[1,128,128]{2,1,0:T(8,128)(2,1)S(1)}, u32[]{:S(2)}, u32[]{:S(2)}) collective-permute-start(bf16[1,128,128]{2,1,0:T(8,128)(2,1)S(1)} %collective-permute-done.15), channel_id=1, source_target_pairs={{0,30},{2,0},{4,2},{6,4},{8,6},{10,8},{12,10},{14,12},{16,14},{18,... | collective-permute-start | bytes 98312 | tf_op jit(solution)/shard_map/ppermute | solution.py:34
  132.4 7.5 %collective-permute-start.18 = (bf16[1,128,128]{2,1,0:T(8,128)(2,1)S(1)}, bf16[1,128,128]{2,1,0:T(8,128)(2,1)S(1)}, u32[]{:S(2)}, u32[]{:S(2)}) collective-permute-start(bf16[1,128,128]{2,1,0:T(8,128)(2,1)S(1)} %collective-permute-done.16), channel_id=1, source_target_pairs={{0,2},{2,4},{4,6},{6,8},{8,10},{10,12},{12,14},{14,16},{16,18},{18... | collective-permute-start | bytes 98312 | tf_op jit(solution)/shard_map/ppermute | solution.py:32
  132.4 7.5 %collective-permute-start.19 = (bf16[1,128,128]{2,1,0:T(8,128)(2,1)S(1)}, bf16[1,128,128]{2,1,0:T(8,128)(2,1)S(1)}, u32[]{:S(2)}, u32[]{:S(2)}) collective-permute-start(bf16[1,128,128]{2,1,0:T(8,128)(2,1)S(1)} %collective-permute-done.17), channel_id=1, source_target_pairs={{0,30},{2,0},{4,2},{6,4},{8,6},{10,8},{12,10},{14,12},{16,14},{18,... | collective-permute-start | bytes 98312 | tf_op jit(solution)/shard_map/ppermute | solution.py:34
  139.9 7.5 %collective-permute-start.20 = (bf16[1,128,128]{2,1,0:T(8,128)(2,1)S(1)}, bf16[1,128,128]{2,1,0:T(8,128)(2,1)S(1)}, u32[]{:S(2)}, u32[]{:S(2)}) collective-permute-start(bf16[1,128,128]{2,1,0:T(8,128)(2,1)S(1)} %collective-permute-done.18), channel_id=1, source_target_pairs={{0,2},{2,4},{4,6},{6,8},{8,10},{10,12},{12,14},{14,16},{16,18},{18... | collective-permute-start | bytes 98312 | tf_op jit(solution)/shard_map/ppermute | solution.py:32
  139.9 7.5 %collective-permute-start.21 = (bf16[1,128,128]{2,1,0:T(8,128)(2,1)S(1)}, bf16[1,128,128]{2,1,0:T(8,128)(2,1)S(1)}, u32[]{:S(2)}, u32[]{:S(2)}) collective-permute-start(bf16[1,128,128]{2,1,0:T(8,128)(2,1)S(1)} %collective-permute-done.19), channel_id=1, source_target_pairs={{0,30},{2,0},{4,2},{6,4},{8,6},{10,8},{12,10},{14,12},{16,14},{18,... | collective-permute-start | bytes 98312 | tf_op jit(solution)/shard_map/ppermute | solution.py:34
  147.4 7.5 %collective-permute-start.22 = (bf16[1,128,128]{2,1,0:T(8,128)(2,1)S(1)}, bf16[1,128,128]{2,1,0:T(8,128)(2,1)S(1)}, u32[]{:S(2)}, u32[]{:S(2)}) collective-permute-start(bf16[1,128,128]{2,1,0:T(8,128)(2,1)S(1)} %collective-permute-done.20), channel_id=1, source_target_pairs={{0,2},{2,4},{4,6},{6,8},{8,10},{10,12},{12,14},{14,16},{16,18},{18... | collective-permute-start | bytes 98312 | tf_op jit(solution)/shard_map/ppermute | solution.py:32
  147.5 7.5 %collective-permute-start.23 = (bf16[1,128,128]{2,1,0:T(8,128)(2,1)S(1)}, bf16[1,128,128]{2,1,0:T(8,128)(2,1)S(1)}, u32[]{:S(2)}, u32[]{:S(2)}) collective-permute-start(bf16[1,128,128]{2,1,0:T(8,128)(2,1)S(1)} %collective-permute-done.21), channel_id=1, source_target_pairs={{0,30},{2,0},{4,2},{6,4},{8,6},{10,8},{12,10},{14,12},{16,14},{18,... | collective-permute-start | bytes 98312 | tf_op jit(solution)/shard_map/ppermute | solution.py:34
  154.9 7.5 %collective-permute-start.24 = (bf16[1,128,128]{2,1,0:T(8,128)(2,1)S(1)}, bf16[1,128,128]{2,1,0:T(8,128)(2,1)S(1)}, u32[]{:S(2)}, u32[]{:S(2)}) collective-permute-start(bf16[1,128,128]{2,1,0:T(8,128)(2,1)S(1)} %collective-permute-done.22), channel_id=1, source_target_pairs={{0,2},{2,4},{4,6},{6,8},{8,10},{10,12},{12,14},{14,16},{16,18},{18... | collective-permute-start | bytes 98312 | tf_op jit(solution)/shard_map/ppermute | solution.py:32
  155.0 7.5 %collective-permute-start.25 = (bf16[1,128,128]{2,1,0:T(8,128)(2,1)S(1)}, bf16[1,128,128]{2,1,0:T(8,128)(2,1)S(1)}, u32[]{:S(2)}, u32[]{:S(2)}) collective-permute-start(bf16[1,128,128]{2,1,0:T(8,128)(2,1)S(1)} %collective-permute-done.23), channel_id=1, source_target_pairs={{0,30},{2,0},{4,2},{6,4},{8,6},{10,8},{12,10},{14,12},{16,14},{18,... | collective-permute-start | bytes 98312 | tf_op jit(solution)/shard_map/ppermute | solution.py:34
  162.5 7.5 %collective-permute-start.26 = (bf16[1,128,128]{2,1,0:T(8,128)(2,1)S(1)}, bf16[1,128,128]{2,1,0:T(8,128)(2,1)S(1)}, u32[]{:S(2)}, u32[]{:S(2)}) collective-permute-start(bf16[1,128,128]{2,1,0:T(8,128)(2,1)S(1)} %collective-permute-done.24), channel_id=1, source_target_pairs={{0,2},{2,4},{4,6},{6,8},{8,10},{10,12},{12,14},{14,16},{16,18},{18... | collective-permute-start | bytes 98312 | tf_op jit(solution)/shard_map/ppermute | solution.py:32
  162.5 15.1 %collective-permute-start.27 = (bf16[1,128,128]{2,1,0:T(8,128)(2,1)S(1)}, bf16[1,128,128]{2,1,0:T(8,128)(2,1)S(1)}, u32[]{:S(2)}, u32[]{:S(2)}) collective-permute-start(bf16[1,128,128]{2,1,0:T(8,128)(2,1)S(1)} %collective-permute-done.25), channel_id=1, source_target_pairs={{0,30},{2,0},{4,2},{6,4},{8,6},{10,8},{12,10},{14,12},{16,14},{18,... | collective-permute-start | bytes 98312 | tf_op jit(solution)/shard_map/ppermute | solution.py:34
  170.0 7.5 %collective-permute-start.28 = (bf16[1,128,128]{2,1,0:T(8,128)(2,1)S(1)}, bf16[1,128,128]{2,1,0:T(8,128)(2,1)S(1)}, u32[]{:S(2)}, u32[]{:S(2)}) collective-permute-start(bf16[1,128,128]{2,1,0:T(8,128)(2,1)S(1)} %collective-permute-done.26), channel_id=1, source_target_pairs={{0,2},{2,4},{4,6},{6,8},{8,10},{10,12},{12,14},{14,16},{16,18},{18... | collective-permute-start | bytes 98312 | tf_op jit(solution)/shard_map/ppermute | solution.py:32
  177.5 7.5 %collective-permute-start.29 = (bf16[1,128,128]{2,1,0:T(8,128)(2,1)S(1)}, bf16[1,128,128]{2,1,0:T(8,128)(2,1)S(1)}, u32[]{:S(2)}, u32[]{:S(2)}) collective-permute-start(bf16[1,128,128]{2,1,0:T(8,128)(2,1)S(1)} %collective-permute-done.28), channel_id=1, source_target_pairs={{0,2},{2,4},{4,6},{6,8},{8,10},{10,12},{12,14},{14,16},{16,18},{18... | collective-permute-start | bytes 98312 | tf_op jit(solution)/shard_map/ppermute | solution.py:32
Sparse Core Ops, SparseCore 0:
  9.7 20.9 all-reduce.2
  101.0 14.1 all-reduce.4
